TPU v7x, 32 devices: a whole 2x2x4 slice. The times are simulated.
32 devices in a mesh: group: 2 (over y), site: 4 (over z), inner: 4 (over x, core).
Axes of the slice: x: 2, y: 2, z: 4, core: 2. Of those that a mesh axis runs over, the one named last changes fastest.
Arguments:
- activations: bfloat16 [8, 384, 2560], P(('group', 'site'), None, 'inner'), parts along dimension 0, may hold values from -6 to 6
- out_grads: bfloat16 [8, 384, 1024], P(('group', 'site')), parts along dimension 0, may hold values from -6 to 6
- site_weights: bfloat16 [8, 1024, 2560], P(('group', 'site'), None, 'inner'), parts along dimension 0, may hold values from -6 to 6
Outputs:
- merged: float32 [2048, 2560], P(('group', 'site'), 'inner'), parts along dimension 0
There are 2 independent parts, one for each index of `group`. A program takes and returns all parts, laid end to end along the dimension named above; each array names one. Nothing has to cross between parts.
All inputs are finite; a program needn't handle non-finite values.
Results may differ from a plain program's by a relative error of at most 0.0003.
Values sent between devices are 32-bit elements; how exact they have to be, the bound alone decides.
No kernel may reach another device: no remote copies, remote signals or barrier semaphores. Data moves between devices by JAX's collectives and lax.ppermute only.
A program may use at most 64 MiB of HBM per device.

v0:
```python
import jax
import jax.numpy as jnp
from jax import lax
from jax.sharding import PartitionSpec as P

ITERS = 4
damping = 1.0
highest = lax.Precision.HIGHEST


def local_term(columns, inputs, grads):
    count = inputs.shape[0]
    in_float = inputs.astype(jnp.float32)
    grad_float = grads.astype(jnp.float32)
    left_prod = jnp.dot(grad_float, columns, precision=highest)
    partial_value = jnp.dot(left_prod, in_float.T, precision=highest)
    token_pair = lax.psum(partial_value, "inner")
    mixed = (
        jnp.dot(token_pair, in_float, precision=highest) / (count * count)
        + damping * left_prod / count
    )
    return jnp.dot(grad_float.T, mixed, precision=highest)


def combine(term):
    return lax.psum_scatter(term, "site", scatter_dimension=0, tiled=True)


def spread(vector):
    return lax.all_gather(vector, "site", axis=0, tiled=True)


def apply_operator(vector, inputs, grads):
    return combine(local_term(spread(vector), inputs, grads))


def square_sum(residual):
    return lax.psum(jnp.sum(residual * residual), ("site", "inner"))


def per_device(activations, out_grads, site_weights):
    inputs = activations[0]
    grads = out_grads[0]
    rhs = combine(local_term(site_weights[0].astype(jnp.float32), inputs, grads))
    merged = jnp.zeros_like(rhs)
    residual = rhs
    direction = rhs
    norm_now = square_sum(residual)
    for count_step in range(ITERS):
        image = apply_operator(direction, inputs, grads)
        inner_prod = lax.psum(jnp.sum(direction * image), ("site", "inner"))
        alpha = norm_now / inner_prod
        merged = merged + alpha * direction
        residual = residual - alpha * image
        norm_next = square_sum(residual)
        direction = residual + norm_next / norm_now * direction
        norm_now = norm_next
    return merged


def solution(mesh):
    return jax.shard_map(
        per_device,
        mesh=mesh,
        in_specs=(
            P(("group", "site"), None, "inner"),
            P(("group", "site"), None, None),
            P(("group", "site"), None, "inner"),
        ),
        out_specs=P(("group", "site"), "inner"),
        check_vma=False,
    )
```

profile of v0, /device:TPU:0, one launch (start us, length us, event | category | flops | bytes accessed | tf_op | source)
XLA Modules:
  0.0 975.9 jit_solution(10916573341953800317)
XLA Ops:
  12.6 36.3 %all-reduce.7.cloned.1.call-done = f32[384,384]{1,0:T(8,128)} async-done(((f32[384,384]{1,0:T(8,128)}), f32[384,384]{1,0:T(8,128)}) %all-reduce.7.cloned.1.call-update) | async-done | bytes 589840 | tf_op jit(solution)/shard_map/psum | solution.py:17
  51.3 3.7 convolution_bitcast_fusion.4
  55.2 52.2 %reduce-scatter.6.cloned.1.call-done = f32[256,640]{0,1:T(8,128)} async-done(((f32[1024,640]{0,1:T(8,128)}), f32[256,640]{0,1:T(8,128)}) %reduce-scatter.6.cloned.1.call-update) | async-done | bytes 655376 | tf_op jit(solution)/shard_map/reduce_scatter | solution.py:26
  107.4 56.0 %all-gather.5.cloned.1.call-done = f32[1024,640]{0,1:T(8,128)} async-done(((f32[256,640]{0,1:T(8,128)}), f32[1024,640]{0,1:T(8,128)}) %all-gather.5.cloned.1.call-update) | async-done | bytes 2621456 | tf_op jit(solution)/shard_map/all_gather | solution.py:30
  163.4 3.9 fusion.17
  174.0 29.4 %all-reduce.9.cloned.1.call-done = f32[384,384]{1,0:T(8,128)} async-done(((f32[384,384]{1,0:T(8,128)}), f32[384,384]{1,0:T(8,128)}) %all-reduce.9.cloned.1.call-update) | async-done | bytes 589840 | tf_op jit(solution)/shard_map/psum | solution.py:17
  205.8 3.7 convolution_bitcast_fusion.3
  209.6 52.2 %reduce-scatter.8.cloned.1.call-done = f32[256,640]{0,1:T(8,128)} async-done(((f32[1024,640]{0,1:T(8,128)}), f32[256,640]{0,1:T(8,128)}) %reduce-scatter.8.cloned.1.call-update) | async-done | bytes 655376 | tf_op jit(solution)/shard_map/reduce_scatter | solution.py:26
  263.8 32.5 %all-reduce = (f32[]{:T(128)}, f32[]{:T(128)}) all-reduce(f32[]{:T(128)} %get-tuple-element.6, f32[]{:T(128)} %get-tuple-element.5), channel_id=1, replica_groups=mesh['group'=2,'site'=4,'inner'=4] {'site','inner'}, use_global_device_ids=true, to_apply=%region_3.0 | all-reduce | flops 2 | bytes 16 | tf_op jit(solution)/shard_map/psum | solution.py:38
  299.4 30.1 %psum.95 = f32[]{:T(128)} all-reduce(f32[]{:T(128)} %multiply_reduce_fusion.5), channel_id=1, replica_groups=mesh['group'=2,'site'=4,'inner'=4] {'site','inner'}, use_global_device_ids=true, to_apply=%region_9.0 | all-reduce | flops 1 | bytes 8 | tf_op jit(solution)/shard_map/psum | solution.py:38
  332.7 52.1 %all-gather.7.cloned.1.call-done = f32[1024,640]{0,1:T(8,128)} async-done(((f32[256,640]{0,1:T(8,128)}), f32[1024,640]{0,1:T(8,128)}) %all-gather.7.cloned.1.call-update) | async-done | bytes 2621456 | tf_op jit(solution)/shard_map/all_gather | solution.py:30
  384.8 3.9 fusion.14
  389.7 2.6 fusion.28
  394.9 29.9 %all-reduce.11.cloned.1.call-done = f32[384,384]{1,0:T(8,128)} async-done(((f32[384,384]{1,0:T(8,128)}), f32[384,384]{1,0:T(8,128)}) %all-reduce.11.cloned.1.call-update) | async-done | bytes 589840 | tf_op jit(solution)/shard_map/psum | solution.py:17
  427.2 3.7 convolution_bitcast_fusion.2
  431.0 52.2 %reduce-scatter.10.cloned.1.call-done = f32[256,640]{0,1:T(8,128)} async-done(((f32[1024,640]{0,1:T(8,128)}), f32[256,640]{0,1:T(8,128)}) %reduce-scatter.10.cloned.1.call-update) | async-done | bytes 655376 | tf_op jit(solution)/shard_map/reduce_scatter | solution.py:26
  485.3 32.5 %psum.97 = f32[]{:T(128)} all-reduce(f32[]{:T(128)} %multiply_reduce_fusion.4), channel_id=1, replica_groups=mesh['group'=2,'site'=4,'inner'=4] {'site','inner'}, use_global_device_ids=true, to_apply=%region_13.0 | all-reduce | flops 1 | bytes 8 | tf_op jit(solution)/shard_map/psum | solution.py:51
  519.0 2.9 multiply_reduce_fusion.3
  521.9 30.1 %psum.98 = f32[]{:T(128)} all-reduce(f32[]{:T(128)} %get-tuple-element.9), channel_id=1, replica_groups=mesh['group'=2,'site'=4,'inner'=4] {'site','inner'}, use_global_device_ids=true, to_apply=%region_15.0 | all-reduce | flops 1 | bytes 8 | tf_op jit(solution)/shard_map/psum | solution.py:38
  555.6 52.1 %all-gather.9.cloned.1.call-done = f32[1024,640]{0,1:T(8,128)} async-done(((f32[256,640]{0,1:T(8,128)}), f32[1024,640]{0,1:T(8,128)}) %all-gather.9.cloned.1.call-update) | async-done | bytes 2621456 | tf_op jit(solution)/shard_map/all_gather | solution.py:30
  607.7 3.9 fusion.11
  617.8 29.9 %all-reduce.13.cloned.1.call-done = f32[384,384]{1,0:T(8,128)} async-done(((f32[384,384]{1,0:T(8,128)}), f32[384,384]{1,0:T(8,128)}) %all-reduce.13.cloned.1.call-update) | async-done | bytes 589840 | tf_op jit(solution)/shard_map/psum | solution.py:17
  650.0 3.7 convolution_bitcast_fusion.1
  653.9 52.2 %reduce-scatter.12.cloned.1.call-done = f32[256,640]{0,1:T(8,128)} async-done(((f32[1024,640]{0,1:T(8,128)}), f32[256,640]{0,1:T(8,128)}) %reduce-scatter.12.cloned.1.call-update) | async-done | bytes 655376 | tf_op jit(solution)/shard_map/reduce_scatter | solution.py:26
  708.2 32.5 %psum.100 = f32[]{:T(128)} all-reduce(f32[]{:T(128)} %multiply_reduce_fusion.2), channel_id=1, replica_groups=mesh['group'=2,'site'=4,'inner'=4] {'site','inner'}, use_global_device_ids=true, to_apply=%region_19.0 | all-reduce | flops 1 | bytes 8 | tf_op jit(solution)/shard_map/psum | solution.py:51
  744.2 30.1 %psum.101 = f32[]{:T(128)} all-reduce(f32[]{:T(128)} %multiply_reduce_fusion.1), channel_id=1, replica_groups=mesh['group'=2,'site'=4,'inner'=4] {'site','inner'}, use_global_device_ids=true, to_apply=%region_21.0 | all-reduce | flops 1 | bytes 8 | tf_op jit(solution)/shard_map/psum | solution.py:38
  778.3 51.9 %all-gather.11.cloned.1.call-done = f32[1024,640]{0,1:T(8,128)} async-done(((f32[256,640]{0,1:T(8,128)}), f32[1024,640]{0,1:T(8,128)}) %all-gather.11.cloned.1.call-update) | async-done | bytes 2621456 | tf_op jit(solution)/shard_map/all_gather | solution.py:30
  830.2 3.9 fusion.8
  840.3 29.9 %all-reduce.15.cloned.1.call-done = f32[384,384]{1,0:T(8,128)} async-done(((f32[384,384]{1,0:T(8,128)}), f32[384,384]{1,0:T(8,128)}) %all-reduce.15.cloned.1.call-update) | async-done | bytes 589840 | tf_op jit(solution)/shard_map/psum | solution.py:17
  872.6 3.7 convolution_bitcast_fusion
  876.4 52.3 %reduce-scatter.14.cloned.1.call-done = f32[256,640]{0,1:T(8,128)} async-done(((f32[1024,640]{0,1:T(8,128)}), f32[256,640]{0,1:T(8,128)}) %reduce-scatter.14.cloned.1.call-update) | async-done | bytes 655376 | tf_op jit(solution)/shard_map/reduce_scatter | solution.py:26
  930.8 32.6 %psum.103 = f32[]{:T(128)} all-reduce(f32[]{:T(128)} %multiply_reduce_fusion), channel_id=1, replica_groups=mesh['group'=2,'site'=4,'inner'=4] {'site','inner'}, use_global_device_ids=true, to_apply=%region_25.0 | all-reduce | flops 1 | bytes 8 | tf_op jit(solution)/shard_map/psum | solution.py:51
  (73 shorter events, 64.4 us)
Async XLA Ops:
  6.5 1.3 copy-start
  6.5 4.2 copy-start.2
  6.5 42.4 %all-reduce.7.cloned.1.call-start = ((), (), s32[]{:S(2)}) async-start(), calls=%async_computation.5 | async-start | bytes 1179648 | tf_op jit(solution)/shard_map/psum | solution.py:17
  9.8 1.0 copy-start.9
  10.7 40.6 %copy-start.1 = (bf16[1,384,1024]{2,1,0:T(8,128)(2,1)S(1)}, bf16[1,384,1024]{2,1,0:T(8,128)(2,1)}, u32[]{:S(2)}) copy-start(bf16[1,384,1024]{2,1,0:T(8,128)(2,1)} %param.4) | copy-start | bytes 2359300
  12.6 94.8 %reduce-scatter.6.cloned.1.call-start = ((), (), s32[]{:S(2)}) async-start(), calls=%async_computation.6 | async-start | bytes 3276800 | tf_op jit(solution)/shard_map/reduce_scatter | solution.py:26
  55.1 108.3 %all-gather.5.cloned.1.call-start = ((), (), s32[]{:S(2)}) async-start(), calls=%async_computation.7 | async-start | bytes 3276800 | tf_op jit(solution)/shard_map/all_gather | solution.py:30
  107.4 96.0 %all-reduce.9.cloned.1.call-start = ((), (), s32[]{:S(2)}) async-start(), calls=%async_computation.8 | async-start | bytes 1179648 | tf_op jit(solution)/shard_map/psum | solution.py:17
  167.4 1.0 copy-start.5
  170.9 90.9 %reduce-scatter.8.cloned.1.call-start = ((), (), s32[]{:S(2)}) async-start(), calls=%async_computation.9 | async-start | bytes 3276800 | tf_op jit(solution)/shard_map/reduce_scatter | solution.py:26
  205.8 56.0 %copy-start.3 = (f32[256,640]{0,1:T(8,128)S(1)}, f32[256,640]{0,1:T(8,128)}, u32[]{:S(2)}) copy-start(f32[256,640]{0,1:T(8,128)} %reduce-scatter.6.cloned.1.call-done) | copy-start | bytes 1966084
  209.6 175.3 %all-gather.7.cloned.1.call-start = ((), (), s32[]{:S(2)}) async-start(), calls=%async_computation.10 | async-start | bytes 3276800 | tf_op jit(solution)/shard_map/all_gather | solution.py:30
  332.7 92.1 %all-reduce.11.cloned.1.call-start = ((), (), s32[]{:S(2)}) async-start(), calls=%async_computation.11 | async-start | bytes 1179648 | tf_op jit(solution)/shard_map/psum | solution.py:17
  388.8 1.0 copy-start.6
  392.4 90.9 %reduce-scatter.10.cloned.1.call-start = ((), (), s32[]{:S(2)}) async-start(), calls=%async_computation.12 | async-start | bytes 3276800 | tf_op jit(solution)/shard_map/reduce_scatter | solution.py:26
  431.0 176.7 %all-gather.9.cloned.1.call-start = ((), (), s32[]{:S(2)}) async-start(), calls=%async_computation.13 | async-start | bytes 3276800 | tf_op jit(solution)/shard_map/all_gather | solution.py:30
  555.5 92.1 %all-reduce.13.cloned.1.call-start = ((), (), s32[]{:S(2)}) async-start(), calls=%async_computation.14 | async-start | bytes 1179648 | tf_op jit(solution)/shard_map/psum | solution.py:17
  611.6 1.0 copy-start.7
  615.2 90.9 %reduce-scatter.12.cloned.1.call-start = ((), (), s32[]{:S(2)}) async-start(), calls=%async_computation.15 | async-start | bytes 3276800 | tf_op jit(solution)/shard_map/reduce_scatter | solution.py:26
  653.8 176.4 %all-gather.11.cloned.1.call-start = ((), (), s32[]{:S(2)}) async-start(), calls=%async_computation.16 | async-start | bytes 3276800 | tf_op jit(solution)/shard_map/all_gather | solution.py:30
  778.1 92.1 %all-reduce.15.cloned.1.call-start = ((), (), s32[]{:S(2)}) async-start(), calls=%async_computation.17 | async-start | bytes 1179648 | tf_op jit(solution)/shard_map/psum | solution.py:17
  834.2 1.0 copy-start.8
  837.7 90.9 %reduce-scatter.14.cloned.1.call-start = ((), (), s32[]{:S(2)}) async-start(), calls=%async_computation.18 | async-start | bytes 3276800 | tf_op jit(solution)/shard_map/reduce_scatter | solution.py:26
  876.3 88.4 %copy-start.4 = (f32[256,640]{0,1:T(8,128)S(1)}, f32[256,640]{0,1:T(8,128)}, u32[]{:S(2)}) copy-start(f32[256,640]{0,1:T(8,128)} %multiply_add_fusion.3) | copy-start | bytes 1966084
Sparse Core Ops, SparseCore 0:
  12.7 36.1 all-reduce.6
  55.2 52.0 reduce-scatter.5
  108.9 54.4 all-gather.4
  171.1 32.2 all-reduce.8
  209.7 52.0 reduce-scatter.7
  332.8 51.9 all-gather.6
  392.5 32.2 all-reduce.10
  431.1 52.0 reduce-scatter.9
  555.7 51.9 all-gather.8
  615.3 32.2 all-reduce.12
  653.9 52.0 reduce-scatter.11
  778.2 51.9 all-gather.10
  837.9 32.2 all-reduce.14
  876.5 52.0 reduce-scatter.13
where the time goes:
time: 984 us; the launch traced here: 976 us
  waiting for transfers between devices  629 us (64%)
  blocking collectives  220 us (22%)
  matrix products  60.5 us (6%)
  other arithmetic  24.1 us (2%)
  between operations  22.5 us (2%)
  local copies, waits for them, and re-layouts  18.3 us (2%)
    reduce_scatter x5, waiting for transfers between devices, combine(): return lax.psum_scatter(term, 'site', scatter_dimension=0, tiled=True)  261 us
    all_gather x4, waiting for transfers between devices, spread(): return lax.all_gather(vector, 'site', axis=0, tiled=True)  212 us
    psum x5, waiting for transfers between devices, local_term(): token_pair = lax.psum(partial_value, 'inner')  155 us
    psum x4, blocking collectives, square_sum(): return lax.psum(jnp.sum(residual * residual), ('site', 'inner'))  123 us
    psum x3, blocking collectives, per_device(): inner_prod = lax.psum(jnp.sum(direction * image), ('site', 'inner'))  97.6 us
  transfers between devices with their start and end apart: 14, of which 14 were waited for; matrix products, arithmetic and copies ran while one was open for 1% of the time, Pallas kernels for 0%

commit v1 on v0

--- a/solution.py
+++ b/solution.py
@@ -6,6 +6,28 @@
 ITERS = 4
 damping = 1.0
 highest = lax.Precision.HIGHEST
+
+
+def joined_along(blocks, dim):
+    dims = list(blocks.shape[1:])
+    dims[dim] *= blocks.shape[0]
+    return jnp.moveaxis(blocks, 0, dim).reshape(dims)
+
+
+def grow_blocks(value, axis):
+    length = lax.axis_size(axis)
+    blocks = value[None]
+    for level in range(length.bit_length() - 1):
+        distance = 1 << level
+        theirs = lax.ppermute(blocks, axis, [(i, i ^ distance) for i in range(length)])
+        both = jnp.stack([blocks, theirs])
+        upper = lax.axis_index(axis) >> level & 1
+        blocks = jnp.where(upper == 0, both, both[::-1]).reshape(-1, *value.shape)
+    return blocks
+
+
+def doubled_up(shard, axis, dim):
+    return joined_along(grow_blocks(shard, axis), dim)
 
 
 def local_term(columns, inputs, grads):
@@ -27,7 +49,7 @@
 
 
 def spread(vector):
-    return lax.all_gather(vector, "site", axis=0, tiled=True)
+    return doubled_up(vector, "site", 0)
 
 
 def apply_operator(vector, inputs, grads):

time: 984 us -> 1100 us (1.12)
  waiting for transfers between devices: 629 us -> 713 us
    ppermute x0 -> x8, waiting for transfers between devices: none -> 298 us  [grow_blocks(): lax.ppermute(blocks, axis, [(i, i ^ distance) for i in range(length)])]
    all_gather x4 -> x0, waiting for transfers between devices: 212 us -> none  [spread(): return lax.all_gather(vector, 'site', axis=0, tiled=True)]
    select_n x0 -> x4, local copies, waits for them, and re-layouts: none -> 13 us  [grow_blocks(): blocks = jnp.where(upper == 0, both, both[::-1]).reshape(-1, *value.shape)]
  transfers between devices with their start and end apart: 14 -> 18, of which waited for: 14 -> 18; matrix products, arithmetic and copies ran while one was open for 1% -> 1% of each run, Pallas kernels for 0% -> 0%
where the time goes in v1:
time: 1100 us; the launch traced here: 1090 us
  waiting for transfers between devices  713 us (65%)
  blocking collectives  221 us (20%)
  matrix products  68.3 us (6%)
  other arithmetic  33.5 us (3%)
  local copies, waits for them, and re-layouts  28.2 us (3%)
  between operations  23.1 us (2%)
    ppermute x8, waiting for transfers between devices, grow_blocks(): lax.ppermute(blocks, axis, [(i, i ^ distance) for i in range(length)])  298 us
    reduce_scatter x5, waiting for transfers between devices, combine(): return lax.psum_scatter(term, 'site', scatter_dimension=0, tiled=True)  261 us
    psum x5, waiting for transfers between devices, local_term(): token_pair = lax.psum(partial_value, 'inner')  154 us
    psum x4, blocking collectives, square_sum(): return lax.psum(jnp.sum(residual * residual), ('site', 'inner'))  124 us
    psum x3, blocking collectives, per_device(): inner_prod = lax.psum(jnp.sum(direction * image), ('site', 'inner'))  97.5 us
    dot_general x5, matrix products, local_term(): left_prod = jnp.dot(grad_float, columns, precision=highest)  25.8 us
  transfers between devices with their start and end apart: 18, of which 18 were waited for; matrix products, arithmetic and copies ran while one was open for 1% of the time, Pallas kernels for 0%

profile of v1, /device:TPU:0, one launch (start us, length us, event | category | flops | bytes accessed | tf_op | source)
XLA Modules:
  0.0 1091.0 jit_solution(9450164895850662734)
XLA Ops:
  11.7 36.2 %all-reduce.7.cloned.1.call-done = f32[384,384]{1,0:T(8,128)} async-done(((f32[384,384]{1,0:T(8,128)}), f32[384,384]{1,0:T(8,128)}) %all-reduce.7.cloned.1.call-update) | async-done | bytes 589840 | tf_op jit(solution)/shard_map/psum | solution.py:39
  50.0 3.7 convolution_bitcast_fusion.4
  54.0 52.0 %reduce-scatter.6.cloned.1.call-done = f32[256,640]{0,1:T(8,128)} async-done(((f32[1024,640]{0,1:T(8,128)}), f32[256,640]{0,1:T(8,128)}) %reduce-scatter.6.cloned.1.call-update) | async-done | bytes 655376 | tf_op jit(solution)/shard_map/reduce_scatter | solution.py:48
  106.7 15.9 %collective-permute-done = f32[1,256,640]{1,2,0:T(8,128)S(1)} collective-permute-done((f32[1,256,640]{1,2,0:T(8,128)}, f32[1,256,640]{1,2,0:T(8,128)S(1)}, u32[]{:S(2)}, u32[]{:S(2)}) %collective-permute-start) | collective-permute-done | bytes 655392 | tf_op jit(solution)/shard_map/ppermute | solution.py:22
  127.3 56.4 %collective-permute-done.1 = f32[2,256,640]{1,2,0:T(8,128)} collective-permute-done((f32[2,256,640]{1,2,0:T(8,128)}, f32[2,256,640]{1,2,0:T(8,128)}, u32[]{:S(2)}, u32[]{:S(2)}) %collective-permute-start.1) | collective-permute-done | bytes 1310752 | tf_op jit(solution)/shard_map/ppermute | solution.py:22
  190.3 6.0 fusion.25
  200.2 32.3 %all-reduce.9.cloned.1.call-done = f32[384,384]{1,0:T(8,128)} async-done(((f32[384,384]{1,0:T(8,128)}), f32[384,384]{1,0:T(8,128)}) %all-reduce.9.cloned.1.call-update) | async-done | bytes 589840 | tf_op jit(solution)/shard_map/psum | solution.py:39
  234.9 3.7 convolution_bitcast_fusion.3
  238.7 52.2 %reduce-scatter.8.cloned.1.call-done = f32[256,640]{0,1:T(8,128)} async-done(((f32[1024,640]{0,1:T(8,128)}), f32[256,640]{0,1:T(8,128)}) %reduce-scatter.8.cloned.1.call-update) | async-done | bytes 655376 | tf_op jit(solution)/shard_map/reduce_scatter | solution.py:48
  292.9 32.6 %all-reduce = (f32[]{:T(128)}, f32[]{:T(128)}) all-reduce(f32[]{:T(128)} %get-tuple-element.6, f32[]{:T(128)} %get-tuple-element.5), channel_id=1, replica_groups=mesh['group'=2,'site'=4,'inner'=4] {'site','inner'}, use_global_device_ids=true, to_apply=%region_3.0 | all-reduce | flops 2 | bytes 16 | tf_op jit(solution)/shard_map/psum | solution.py:60
  328.7 30.3 %psum.95 = f32[]{:T(128)} all-reduce(f32[]{:T(128)} %multiply_reduce_fusion.5), channel_id=1, replica_groups=mesh['group'=2,'site'=4,'inner'=4] {'site','inner'}, use_global_device_ids=true, to_apply=%region_9.10 | all-reduce | flops 1 | bytes 8 | tf_op jit(solution)/shard_map/psum | solution.py:60
  361.6 16.5 %collective-permute-done.2 = f32[1,256,640]{1,2,0:T(8,128)S(1)} collective-permute-done((f32[1,256,640]{1,2,0:T(8,128)S(1)}, f32[1,256,640]{1,2,0:T(8,128)S(1)}, u32[]{:S(2)}, u32[]{:S(2)}) %collective-permute-start.2) | collective-permute-done | bytes 655392 | tf_op jit(solution)/shard_map/ppermute | solution.py:22
  378.4 58.7 %collective-permute-done.3 = f32[2,256,640]{1,2,0:T(8,128)S(1)} collective-permute-done((f32[2,256,640]{1,2,0:T(8,128)S(1)}, f32[2,256,640]{1,2,0:T(8,128)S(1)}, u32[]{:S(2)}, u32[]{:S(2)}) %collective-permute-start.3) | collective-permute-done | bytes 1310752 | tf_op jit(solution)/shard_map/ppermute | solution.py:22
  442.3 6.0 fusion.22
  454.4 28.5 %all-reduce.11.cloned.1.call-done = f32[384,384]{1,0:T(8,128)} async-done(((f32[384,384]{1,0:T(8,128)}), f32[384,384]{1,0:T(8,128)}) %all-reduce.11.cloned.1.call-update) | async-done | bytes 589840 | tf_op jit(solution)/shard_map/psum | solution.py:39
  489.1 52.2 %reduce-scatter.10.cloned.1.call-done = f32[256,640]{0,1:T(8,128)} async-done(((f32[1024,640]{0,1:T(8,128)}), f32[256,640]{0,1:T(8,128)}) %reduce-scatter.10.cloned.1.call-update) | async-done | bytes 655376 | tf_op jit(solution)/shard_map/reduce_scatter | solution.py:48
  543.2 32.5 %psum.97 = f32[]{:T(128)} all-reduce(f32[]{:T(128)} %multiply_reduce_fusion.4), channel_id=1, replica_groups=mesh['group'=2,'site'=4,'inner'=4] {'site','inner'}, use_global_device_ids=true, to_apply=%region_13.14 | all-reduce | flops 1 | bytes 8 | tf_op jit(solution)/shard_map/psum | solution.py:73
  579.8 30.6 %psum.98 = f32[]{:T(128)} all-reduce(f32[]{:T(128)} %get-tuple-element.9), channel_id=1, replica_groups=mesh['group'=2,'site'=4,'inner'=4] {'site','inner'}, use_global_device_ids=true, to_apply=%region_15.16 | all-reduce | flops 1 | bytes 8 | tf_op jit(solution)/shard_map/psum | solution.py:60
  612.9 16.5 %collective-permute-done.4 = f32[1,256,640]{1,2,0:T(8,128)S(1)} collective-permute-done((f32[1,256,640]{1,2,0:T(8,128)S(1)}, f32[1,256,640]{1,2,0:T(8,128)S(1)}, u32[]{:S(2)}, u32[]{:S(2)}) %collective-permute-start.4) | collective-permute-done | bytes 655392 | tf_op jit(solution)/shard_map/ppermute | solution.py:22
  629.8 58.7 %collective-permute-done.5 = f32[2,256,640]{1,2,0:T(8,128)S(1)} collective-permute-done((f32[2,256,640]{1,2,0:T(8,128)S(1)}, f32[2,256,640]{1,2,0:T(8,128)S(1)}, u32[]{:S(2)}, u32[]{:S(2)}) %collective-permute-start.5) | collective-permute-done | bytes 1310752 | tf_op jit(solution)/shard_map/ppermute | solution.py:22
  693.7 6.0 fusion.19
  705.8 28.5 %all-reduce.13.cloned.1.call-done = f32[384,384]{1,0:T(8,128)} async-done(((f32[384,384]{1,0:T(8,128)}), f32[384,384]{1,0:T(8,128)}) %all-reduce.13.cloned.1.call-update) | async-done | bytes 589840 | tf_op jit(solution)/shard_map/psum | solution.py:39
  736.7 3.7 convolution_bitcast_fusion.1
  740.5 52.2 %reduce-scatter.12.cloned.1.call-done = f32[256,640]{0,1:T(8,128)} async-done(((f32[1024,640]{0,1:T(8,128)}), f32[256,640]{0,1:T(8,128)}) %reduce-scatter.12.cloned.1.call-update) | async-done | bytes 655376 | tf_op jit(solution)/shard_map/reduce_scatter | solution.py:48
  794.8 32.5 %psum.100 = f32[]{:T(128)} all-reduce(f32[]{:T(128)} %multiply_reduce_fusion.2), channel_id=1, replica_groups=mesh['group'=2,'site'=4,'inner'=4] {'site','inner'}, use_global_device_ids=true, to_apply=%region_19.20 | all-reduce | flops 1 | bytes 8 | tf_op jit(solution)/shard_map/psum | solution.py:73
  830.6 30.3 %psum.101 = f32[]{:T(128)} all-reduce(f32[]{:T(128)} %multiply_reduce_fusion.1), channel_id=1, replica_groups=mesh['group'=2,'site'=4,'inner'=4] {'site','inner'}, use_global_device_ids=true, to_apply=%region_21.22 | all-reduce | flops 1 | bytes 8 | tf_op jit(solution)/shard_map/psum | solution.py:60
  863.9 16.5 %collective-permute-done.6 = f32[1,256,640]{1,2,0:T(8,128)S(1)} collective-permute-done((f32[1,256,640]{1,2,0:T(8,128)S(1)}, f32[1,256,640]{1,2,0:T(8,128)S(1)}, u32[]{:S(2)}, u32[]{:S(2)}) %collective-permute-start.6) | collective-permute-done | bytes 655392 | tf_op jit(solution)/shard_map/ppermute | solution.py:22
  880.8 58.7 %collective-permute-done.7 = f32[2,256,640]{1,2,0:T(8,128)S(1)} collective-permute-done((f32[2,256,640]{1,2,0:T(8,128)S(1)}, f32[2,256,640]{1,2,0:T(8,128)S(1)}, u32[]{:S(2)}, u32[]{:S(2)}) %collective-permute-start.7) | collective-permute-done | bytes 1310752 | tf_op jit(solution)/shard_map/ppermute | solution.py:22
  944.6 6.0 fusion.16
  956.8 28.5 %all-reduce.15.cloned.1.call-done = f32[384,384]{1,0:T(8,128)} async-done(((f32[384,384]{1,0:T(8,128)}), f32[384,384]{1,0:T(8,128)}) %all-reduce.15.cloned.1.call-update) | async-done | bytes 589840 | tf_op jit(solution)/shard_map/psum | solution.py:39
  991.4 52.3 %reduce-scatter.14.cloned.1.call-done = f32[256,640]{0,1:T(8,128)} async-done(((f32[1024,640]{0,1:T(8,128)}), f32[256,640]{0,1:T(8,128)}) %reduce-scatter.14.cloned.1.call-update) | async-done | bytes 655376 | tf_op jit(solution)/shard_map/reduce_scatter | solution.py:48
  1045.8 32.5 %psum.103 = f32[]{:T(128)} all-reduce(f32[]{:T(128)} %multiply_reduce_fusion), channel_id=1, replica_groups=mesh['group'=2,'site'=4,'inner'=4] {'site','inner'}, use_global_device_ids=true, to_apply=%region_25.26 | all-reduce | flops 1 | bytes 8 | tf_op jit(solution)/shard_map/psum | solution.py:73
  (97 shorter events, 98.9 us)
Async XLA Ops:
  6.5 1.3 copy-start
  6.5 3.2 copy-start.3
  6.5 41.4 %all-reduce.7.cloned.1.call-start = ((), (), s32[]{:S(2)}) async-start(), calls=%async_computation.5 | async-start | bytes 1179648 | tf_op jit(solution)/shard_map/psum | solution.py:39
  9.8 40.2 %copy-start.2 = (bf16[1,384,1024]{2,1,0:T(8,128)(2,1)S(1)}, bf16[1,384,1024]{2,1,0:T(8,128)(2,1)}, u32[]{:S(2)}) copy-start(bf16[1,384,1024]{2,1,0:T(8,128)(2,1)} %param.4) | copy-start | bytes 2359300
  11.6 94.4 %reduce-scatter.6.cloned.1.call-start = ((), (), s32[]{:S(2)}) async-start(), calls=%async_computation.6 | async-start | bytes 3276800 | tf_op jit(solution)/shard_map/reduce_scatter | solution.py:48
  53.8 178.7 %all-reduce.9.cloned.1.call-start = ((), (), s32[]{:S(2)}) async-start(), calls=%async_computation.7 | async-start | bytes 1179648 | tf_op jit(solution)/shard_map/psum | solution.py:39
  106.1 16.5 %collective-permute-start = (f32[1,256,640]{1,2,0:T(8,128)}, f32[1,256,640]{1,2,0:T(8,128)S(1)}, u32[]{:S(2)}, u32[]{:S(2)}) collective-permute-start(f32[1,256,640]{1,2,0:T(8,128)} %bitcast.124), channel_id=1, source_target_pairs={{0,4},{4,0},{8,12},{12,8},{1,5},{5,1},{9,13},{13,9},{2,6},{6,2},{1... | collective-permute-start | bytes 1966088 | tf_op jit(solution)/shard_map/ppermute | solution.py:22
  125.0 58.8 %collective-permute-start.1 = (f32[2,256,640]{1,2,0:T(8,128)}, f32[2,256,640]{1,2,0:T(8,128)}, u32[]{:S(2)}, u32[]{:S(2)}) collective-permute-start(f32[2,256,640]{1,2,0:T(8,128)} %get-tuple-element.18), channel_id=1, source_target_pairs={{0,8},{4,12},{8,0},{12,4},{1,9},{5,13},{9,1},{13,5},{2,10},{6,14},... | collective-permute-start | bytes 3932168 | tf_op jit(solution)/shard_map/ppermute | solution.py:22
  198.8 92.1 %reduce-scatter.8.cloned.1.call-start = ((), (), s32[]{:S(2)}) async-start(), calls=%async_computation.8 | async-start | bytes 3276800 | tf_op jit(solution)/shard_map/reduce_scatter | solution.py:48
  234.9 56.0 %copy-start.4 = (f32[256,640]{0,1:T(8,128)S(1)}, f32[256,640]{0,1:T(8,128)}, u32[]{:S(2)}) copy-start(f32[256,640]{0,1:T(8,128)} %reduce-scatter.6.cloned.1.call-done) | copy-start | bytes 1966084
  238.7 244.2 %all-reduce.11.cloned.1.call-start = ((), (), s32[]{:S(2)}) async-start(), calls=%async_computation.9 | async-start | bytes 1179648 | tf_op jit(solution)/shard_map/psum | solution.py:39
  361.5 16.6 %collective-permute-start.2 = (f32[1,256,640]{1,2,0:T(8,128)S(1)}, f32[1,256,640]{1,2,0:T(8,128)S(1)}, u32[]{:S(2)}, u32[]{:S(2)}) collective-permute-start(f32[1,256,640]{1,2,0:T(8,128)S(1)} %bitcast.126), channel_id=1, source_target_pairs={{0,4},{4,0},{8,12},{12,8},{1,5},{5,1},{9,13},{13,9},{2,6},{6,2},{1... | collective-permute-start | bytes 1966088 | tf_op jit(solution)/shard_map/ppermute | solution.py:22
  378.3 58.7 %collective-permute-start.3 = (f32[2,256,640]{1,2,0:T(8,128)S(1)}, f32[2,256,640]{1,2,0:T(8,128)S(1)}, u32[]{:S(2)}, u32[]{:S(2)}) collective-permute-start(f32[2,256,640]{1,2,0:T(8,128)S(1)} %get-tuple-element.16), channel_id=1, source_target_pairs={{0,8},{4,12},{8,0},{12,4},{1,9},{5,13},{9,1},{13,5},{2,10},{6,14},... | collective-permute-start | bytes 3932168 | tf_op jit(solution)/shard_map/ppermute | solution.py:22
  448.3 1.0 copy-start.7
  451.8 89.5 %reduce-scatter.10.cloned.1.call-start = ((), (), s32[]{:S(2)}) async-start(), calls=%async_computation.10 | async-start | bytes 3276800 | tf_op jit(solution)/shard_map/reduce_scatter | solution.py:48
  489.0 245.2 %all-reduce.13.cloned.1.call-start = ((), (), s32[]{:S(2)}) async-start(), calls=%async_computation.11 | async-start | bytes 1179648 | tf_op jit(solution)/shard_map/psum | solution.py:39
  612.8 16.6 %copy-start.5 = (f32[256,640]{0,1:T(8,128)}, f32[256,640]{0,1:T(8,128)S(1)}, u32[]{:S(2)}) copy-start(f32[256,640]{0,1:T(8,128)S(1)} %multiply_add_fusion.2) | copy-start | bytes 1966084
  612.8 16.6 %collective-permute-start.4 = (f32[1,256,640]{1,2,0:T(8,128)S(1)}, f32[1,256,640]{1,2,0:T(8,128)S(1)}, u32[]{:S(2)}, u32[]{:S(2)}) collective-permute-start(f32[1,256,640]{1,2,0:T(8,128)S(1)} %bitcast.128), channel_id=1, source_target_pairs={{0,4},{4,0},{8,12},{12,8},{1,5},{5,1},{9,13},{13,9},{2,6},{6,2},{1... | collective-permute-start | bytes 1966088 | tf_op jit(solution)/shard_map/ppermute | solution.py:22
  629.7 58.7 %collective-permute-start.5 = (f32[2,256,640]{1,2,0:T(8,128)S(1)}, f32[2,256,640]{1,2,0:T(8,128)S(1)}, u32[]{:S(2)}, u32[]{:S(2)}) collective-permute-start(f32[2,256,640]{1,2,0:T(8,128)S(1)} %get-tuple-element.14), channel_id=1, source_target_pairs={{0,8},{4,12},{8,0},{12,4},{1,9},{5,13},{9,1},{13,5},{2,10},{6,14},... | collective-permute-start | bytes 3932168 | tf_op jit(solution)/shard_map/ppermute | solution.py:22
  699.6 1.0 copy-start.8
  703.2 89.5 %reduce-scatter.12.cloned.1.call-start = ((), (), s32[]{:S(2)}) async-start(), calls=%async_computation.12 | async-start | bytes 3276800 | tf_op jit(solution)/shard_map/reduce_scatter | solution.py:48
  740.4 244.8 %all-reduce.15.cloned.1.call-start = ((), (), s32[]{:S(2)}) async-start(), calls=%async_computation.13 | async-start | bytes 1179648 | tf_op jit(solution)/shard_map/psum | solution.py:39
  863.8 16.6 %copy-start.6 = (f32[256,640]{0,1:T(8,128)}, f32[256,640]{0,1:T(8,128)S(1)}, u32[]{:S(2)}) copy-start(f32[256,640]{0,1:T(8,128)S(1)} %multiply_add_fusion.1) | copy-start | bytes 1966084
  863.8 16.6 %collective-permute-start.6 = (f32[1,256,640]{1,2,0:T(8,128)S(1)}, f32[1,256,640]{1,2,0:T(8,128)S(1)}, u32[]{:S(2)}, u32[]{:S(2)}) collective-permute-start(f32[1,256,640]{1,2,0:T(8,128)S(1)} %bitcast.134), channel_id=1, source_target_pairs={{0,4},{4,0},{8,12},{12,8},{1,5},{5,1},{9,13},{13,9},{2,6},{6,2},{1... | collective-permute-start | bytes 1966088 | tf_op jit(solution)/shard_map/ppermute | solution.py:22
  880.7 58.7 %collective-permute-start.7 = (f32[2,256,640]{1,2,0:T(8,128)S(1)}, f32[2,256,640]{1,2,0:T(8,128)S(1)}, u32[]{:S(2)}, u32[]{:S(2)}) collective-permute-start(f32[2,256,640]{1,2,0:T(8,128)S(1)} %get-tuple-element.12), channel_id=1, source_target_pairs={{0,8},{4,12},{8,0},{12,4},{1,9},{5,13},{9,1},{13,5},{2,10},{6,14},... | collective-permute-start | bytes 3932168 | tf_op jit(solution)/shard_map/ppermute | solution.py:22
  950.6 1.0 copy-start.9
  954.2 89.5 %reduce-scatter.14.cloned.1.call-start = ((), (), s32[]{:S(2)}) async-start(), calls=%async_computation.14 | async-start | bytes 3276800 | tf_op jit(solution)/shard_map/reduce_scatter | solution.py:48
  1043.7 40.3 %copy-start.1 = (bf16[1,1024,640]{2,1,0:T(8,128)(2,1)S(1)}, bf16[1,1024,640]{2,1,0:T(8,128)(2,1)}, u32[]{:S(2)}) copy-start(bf16[1,1024,640]{2,1,0:T(8,128)(2,1)} %param.5) | copy-start | bytes 3932164
Sparse Core Ops, SparseCore 0:
  11.8 36.1 all-reduce.6
  53.9 52.0 reduce-scatter.5
  199.0 33.4 all-reduce.8
  238.8 52.0 reduce-scatter.7
  451.9 30.8 all-reduce.10
  489.2 52.0 reduce-scatter.9
  703.3 30.8 all-reduce.12
  740.6 52.0 reduce-scatter.11
  954.3 30.8 all-reduce.14
  991.5 52.0 reduce-scatter.13
